TPU v7x, 128 devices: a whole 4x4x4 slice. The times are simulated.
128 devices in a mesh: gx: 8 (over y_hi, z), gy: 16 (over x, y_lo, core).
Axes of the slice: x: 4, y: 4 (y_hi: 2, y_lo: 2; y = y_hi * 2 + y_lo), z: 4, core: 2. Of those that a mesh axis runs over, the one named last changes fastest.
Arguments:
- observed: float32 [2, 8192, 8192], P(None, 'gx', 'gy'), may hold values from -6 to 6
- noise_var: float32 [8192, 8192], P('gx', 'gy'), may hold values from 0.05 to 0.5
- row_kernel: float32 [4096, 4096], P('gx'), may hold values from -1 to 1.2, as said below
- col_kernel: float32 [4096, 4096], P('gy'), may hold values from -1 to 1.2, as said below
Outputs:
- gram_times: float32 [2, 8192, 8192], P(None, 'gx', 'gy')
Inputs may be any that keep to these rules, and one draw needn't show every extreme that they name: row_kernel is symmetric. col_kernel is symmetric.
All inputs are finite; a program needn't handle non-finite values.
Results may differ from a plain program's by a relative error of at most 0.000065.
Values sent between devices are 32-bit elements; how exact they have to be, the bound alone decides.
No kernel may reach another device: no remote copies, remote signals or barrier semaphores. Data moves between devices by JAX's collectives and lax.ppermute only.
A program may use at most 128 MiB of HBM per device.

v0:
```python
import jax
import jax.numpy as jnp
from jax import lax
from jax.sharding import Mesh, PartitionSpec as P


def axis_count(axis):
    return lax.psum(1, axis)


def with_halo(cells, sides, width):
    for axis, dim in sides:
        count = axis_count(axis)
        ends = count - 1
        head = lax.slice_in_dim(cells, 0, width, axis=dim)
        tail = lax.slice_in_dim(cells, cells.shape[dim] - width, cells.shape[dim], axis=dim)
        cells = jnp.concatenate(
            [
                lax.ppermute(tail, axis, [(i, (i + 1) % count) for i in range(ends)]),
                cells,
                lax.ppermute(head, axis, [((i + 1) % count, i) for i in range(ends)]),
            ],
            axis=dim,
        )
    return cells


def edges(cells, axis, dim, width):
    count = axis_count(axis)
    ends = count - 1
    head = lax.slice_in_dim(cells, 0, width, axis=dim)
    tail = lax.slice_in_dim(cells, cells.shape[dim] - width, cells.shape[dim], axis=dim)
    before = lax.ppermute(tail, axis, [(i, i + 1) for i in range(ends)])
    after = lax.ppermute(head, axis, [(i + 1, i) for i in range(ends)])
    return (before, after)


def keys_weight(dist):
    span = jnp.abs(dist)
    inner = (1.5 * span - 2.5) * span * span + 1.0
    outer = ((-0.5 * span + 2.5) * span - 4.0) * span + 2.0
    return jnp.where(span < 1.0, inner, jnp.where(span < 2.0, outer, 0.0))


def tap_table(rows, cols, coarse_on_rows, pad):
    r = lax.broadcasted_iota(jnp.float32, (rows, cols), 0)
    c = lax.broadcasted_iota(jnp.float32, (rows, cols), 1)
    if coarse_on_rows:
        coarse, fine = (r, c)
    else:
        coarse, fine = (c, r)
    if pad == 4:
        dist = coarse - ((fine - 4.0) * 0.5 + 0.25)
    else:
        dist = coarse - 2.0 - (fine * 0.5 + 0.25)
    return keys_weight(dist).astype(jnp.bfloat16)


def split3(x):
    hi = lax.reduce_precision(x, exponent_bits=8, mantissa_bits=7)
    rest = x - hi
    mid = lax.reduce_precision(rest, exponent_bits=8, mantissa_bits=7)
    lo = rest - mid
    return (hi.astype(jnp.bfloat16), mid.astype(jnp.bfloat16), lo.astype(jnp.bfloat16))


def exact_dot(eq, x, table, data_first):
    ins, _ = eq.split("->")
    first, second = ins.split(",")
    if data_first:
        parts = jnp.concatenate(split3(x), axis=first.index(second[0]))
        return jnp.einsum(
            eq, parts, jnp.concatenate([table] * 3, axis=0), preferred_element_type=jnp.float32
        )
    parts = jnp.concatenate(split3(x), axis=second.index(first[1]))
    return jnp.einsum(
        eq, jnp.concatenate([table] * 3, axis=1), parts, preferred_element_type=jnp.float32
    )


def row_windows(kernel, order, block, width):
    padded = jnp.pad(kernel, ((0, width - kernel.shape[0]), (2, width - block - 2)))
    return jnp.concatenate([padded[:, block * w : block * w + width] for w in order], axis=1)


def body(observed, noise_var, row_kernel, col_kernel):
    highest = lax.Precision.HIGH
    rows_axis = ("yh", "z")
    cols_axis = ("x", "yl", "core")
    tile_rows = row_kernel.shape[0]
    tile_cols = col_kernel.shape[0]
    ext_rows = tile_rows + 8
    row_count = axis_count(rows_axis)
    swap = [(0, 1), (1, 0)]
    side = lax.axis_index("yl")
    span = 4 * tile_cols
    quarters = range(col_kernel.shape[1] // span)
    low = jnp.concatenate(
        [col_kernel[:, q * span : q * span + span // 2] for q in quarters], axis=1
    )
    high = jnp.concatenate(
        [col_kernel[:, q * span + span // 2 : (q + 1) * span] for q in quarters], axis=1
    )
    near_cols = jnp.where(side == 0, low, high)
    far_cols = jnp.where(side == 0, high, low)
    partner_cols = lax.ppermute(far_cols, "yl", swap)
    row_rows = with_halo(row_kernel, ((rows_axis, 0),), 2)
    halves_n = axis_count("yh")
    depth = axis_count("z")
    order = [h * depth + d for d in range(depth) for h in range(halves_n)]
    row_big = row_windows(row_rows, order, tile_rows, ext_rows)
    before, after = edges(observed, cols_axis, 2, 4)
    col_adj = tap_table(2 * tile_cols + 8, tile_cols, False, 4)
    row_adj = tap_table(ext_rows, 2 * tile_rows, True, 2)
    colsum = (
        exact_dot("rpq,qj->rpj", observed, col_adj[4:-4], True)
        + exact_dot("rpq,qj->rpj", before, col_adj[:4], True)
        + exact_dot("rpq,qj->rpj", after, col_adj[-4:], True)
    )
    inducing = exact_dot("ip,rpj->rij", colsum, row_adj, False)
    half = lax.all_gather(inducing, ("x", "core"), axis=2, tiled=True)
    near = jnp.einsum("rik,jk->rij", half, near_cols, precision=highest)
    for_partner = jnp.einsum("rik,jk->rij", half, partner_cols, precision=highest)
    mixed = near + lax.ppermute(for_partner, "yl", swap)
    product = jnp.einsum(
        "ik,rkj->rij",
        row_big,
        lax.all_gather(mixed, ("z", "yh"), axis=1, tiled=True),
        precision=highest,
    )
    coarse_ext = with_halo(product, ((cols_axis, 2),), 2)
    row_fwd = tap_table(2 * tile_rows, ext_rows, False, 2)
    col_fwd = tap_table(tile_cols + 4, 2 * tile_cols, True, 2)
    rowpass = exact_dot("pi,rij->rpj", coarse_ext, row_fwd, False)
    result = exact_dot("rpj,jq->rpq", rowpass, col_fwd, True)
    return result + noise_var[None] * observed


def solution(mesh):
    rows_n, cols_n = mesh.devices.shape
    z = min(4, rows_n)
    shape = (rows_n // z, z, cols_n // 4, 2, 2)
    fine = Mesh(mesh.devices.reshape(shape), ("yh", "z", "x", "yl", "core"))
    rows = ("yh", "z")
    cols = ("x", "yl", "core")
    return jax.shard_map(
        body,
        mesh=fine,
        in_specs=(P(None, rows, cols), P(rows, cols), P(rows, None), P(cols, None)),
        out_specs=P(None, rows, cols),
        check_vma=False,
    )
```

profile of v0, /device:TPU:9, one launch (start us, length us, event | category | flops | bytes accessed | tf_op | source)
XLA Modules:
  0.0 259.7 jit_solution(11175421567967225632)
XLA Ops:
  6.5 1.9 fusion.117
  8.8 3.6 %collective-permute-start = (f32[2,1024,4]{1,2,0:T(4,128)S(1)}, f32[2,1024,4]{1,2,0:T(4,128)S(1)}, u32[]{:S(2)}, u32[]{:S(2)}) collective-permute-start(f32[2,1024,4]{1,2,0:T(4,128)S(1)} %copy.16), channel_id=1, source_target_pairs={{0,1},{1,2},{2,3},{3,4},{4,5},{5,6},{6,7},{7,8},{8,9},{9,10},{10,1... | collective-permute-start | bytes 98312 | tf_op jit(solution)/shard_map/ppermute | solution.py:33
  12.7 1.9 collective-permute-start.1
  14.6 3.2 %reduce-precision_convert_fusion.1 = (bf16[2,1024,512]{2,1,0:T(8,128)(2,1)S(1)}, bf16[2,1024,512]{2,1,0:T(8,128)(2,1)S(1)}, bf16[2,1024,512]{2,1,0:T(8,128)(2,1)S(1)}) fusion(f32[2,1024,512]{2,1,0:T(8,128)} %param.4), kind=kLoop, calls=%fused_computation.18 | loop fusion | flops 7340032 | bytes 10485760 | tf_op jit(solution)/shard_map/convert_element_type | solution.py:64
  20.6 2.3 reduce-precision_convert_fusion.5
  22.9 2.8 %fusion.59 = f32[2,520,256]{2,1,0:T(8,128)} fusion(bf16[520,1024]{1,0:T(8,128)(2,1)S(1)} %fusion.40, bf16[2,1024,256]{2,1,0:T(8,128)(2,1)S(1)} %get-tuple-element.35, bf16[2,1024,256]{2,1,0:T(8,128)(2,1)S(1)} %get-tuple-element.36, bf16[2,1024,256]{2,1,0:T(8,128)(2,1)S(1)} %get-tuple-element.34), kind=kOutput, calls=%fused_computation.87 | convolution fusion | flops 1654800384 | bytes 5275648 | tf_op jit(solution)/shard_map/ip,rpj->rij/dot_general | solution.py:76
  25.7 2.6 %fusion.116 = (f32[256,512]{1,0:T(8,128)S(1)}, f32[256,512]{1,0:T(8,128)S(1)}, f32[256,512]{1,0:T(8,128)S(1)}, f32[256,512]{1,0:T(8,128)S(1)}, f32[256,512]{1,0:...) fusion(f32[256,4096]{1,0:T(8,128)} %param.7), kind=kLoop, calls=%fused_computation.161 | loop fusion | bytes 8388608 | tf_op jit(solution)/shard_map/slice | solution.py:99
  29.7 46.2 %collective-permute-done.2 = f32[256,2048]{1,0:T(8,128)} collective-permute-done((f32[256,2048]{1,0:T(8,128)S(1)}, f32[256,2048]{1,0:T(8,128)}, u32[]{:S(2)}, u32[]{:S(2)}) %collective-permute-start.2) | collective-permute-done | bytes 2097184 | tf_op jit(solution)/shard_map/ppermute | solution.py:106
  75.9 3.9 %all-gather.3.cloned.1.call-done = f32[2,520,2048]{2,1,0:T(8,128)} async-done(((f32[2,520,256]{2,1,0:T(8,128)}), f32[2,520,2048]{2,1,0:T(8,128)}) %all-gather.3.cloned.1.call-update) | async-done | bytes 8519696 | tf_op jit(solution)/shard_map/all_gather | solution.py:121
  79.8 6.9 %fusion.49 = f32[2,520,256]{2,1,0:T(8,128)S(1)} fusion(f32[2,520,2048]{2,1,0:T(8,128)} %all-gather.3.cloned.1.call-done, f32[256,2048]{1,0:T(8,128)} %collective-permute-done.2), kind=kOutput, calls=%fused_computation.79 | convolution fusion | flops 3271557120 | bytes 11681792 | tf_op jit(solution)/shard_map/rik,jk->rij/dot_general | solution.py:123
  87.2 3.5 %fusion.51 = f32[2,520,256]{2,1,0:T(8,128)S(1)} fusion(f32[2,520,2048]{2,1,0:T(8,128)S(1)} %copy-done, f32[256,512]{1,0:T(8,128)S(1)} %copy-done.3, f32[256,512]{1,0:T(8,128)S(1)} %copy-done.5, f32[256,512]{1,0:T(8,128)S(1)} %get-tuple-element.16, f32[256,512]{1,0:T(8,128)S(1)} %get-tuple-element.17, f32[256,512]{1,0:T(8,128)S(1)} %get-tuple-element.18, ...), kind=kOutput, calls=%fused_computation.81 | convolution fusion | flops 3275227136 | bytes 13778945 | tf_op jit(solution)/shard_map/rik,jk->rij/dot_general | solution.py:122
  90.7 21.1 %collective-permute-done.3 = f32[2,520,256]{2,1,0:T(8,128)S(1)} collective-permute-done((f32[2,520,256]{2,1,0:T(8,128)S(1)}, f32[2,520,256]{2,1,0:T(8,128)S(1)}, u32[]{:S(2)}, u32[]{:S(2)}) %collective-permute-start.3) | collective-permute-done | bytes 1064992 | tf_op jit(solution)/shard_map/ppermute | solution.py:124
  114.0 3.2 %collective-permute-start.4 = (f32[2,4096]{1,0:T(2,128)S(1)}, f32[2,4096]{1,0:T(2,128)S(1)}, u32[]{:S(2)}, u32[]{:S(2)}) collective-permute-start(f32[2,4096]{1,0:T(2,128)S(1)} %get-tuple-element.13), channel_id=1, source_target_pairs={{0,16},{16,32},{32,48},{48,64},{64,80},{80,96},{96,112},{1,17},{17... | collective-permute-start | bytes 98312 | tf_op jit(solution)/shard_map/ppermute | solution.py:19
  118.5 2.3 fusion.43
  121.8 10.9 %select_maximum_fusion = f32[520,4104]{1,0:T(8,128)S(1)} fusion(f32[2,4096]{1,0:T(2,128)S(1)} %collective-permute-done.5, f32[512,4096]{1,0:T(8,128)} %param.6, f32[2,4096]{1,0:T(2,128)S(1)} %collective-permute-done.4), kind=kLoop, calls=%fused_computation.2 | loop fusion | flops 27743040 | bytes 16990464 | tf_op jit(solution)/shard_map/concatenate | solution.py:17
  132.7 3.4 %fusion.114 = (f32[520,520]{1,0:T(8,128)S(1)}, f32[520,520]{1,0:T(8,128)S(1)}, f32[520,520]{1,0:T(8,128)}, f32[520,520]{1,0:T(8,128)}, f32[520,520]{1,0:T(8,128)...) fusion(f32[520,4104]{1,0:T(8,128)S(1)} %select_maximum_fusion), kind=kLoop, calls=%fused_computation.159 | loop fusion | bytes 17305600 | tf_op jit(solution)/shard_map/slice | solution.py:83
  136.1 11.6 %concatenate.62 = f32[520,4160]{1,0:T(8,128)} concatenate(f32[520,520]{1,0:T(8,128)} %get-tuple-element.12, f32[520,520]{1,0:T(8,128)} %get-tuple-element.11, f32[520,520]{1,0:T(8,128)} %get-tuple-element.10, f32[520,520]{1,0:T(8,128)} %get-tuple-element.9, f32[520,520]{1,0:T(8,128)} %get-tuple-element.8, f32[520,520]{1,0:T(8,128)} %get-tuple-element.7, ...), dimensions={1} | concatenate | bytes 17305600 | tf_op jit(solution)/shard_map/concatenate | solution.py:83
  147.7 73.1 %all-gather.5.cloned.1.call-done = f32[2,4160,256]{2,1,0:T(8,128)} async-done(((f32[2,520,256]{2,1,0:T(8,128)}), f32[2,4160,256]{2,1,0:T(8,128)}) %all-gather.5.cloned.1.call-update) | async-done | bytes 8519696 | tf_op jit(solution)/shard_map/all_gather | solution.py:128
  220.9 12.2 %fusion.62 = f32[2,520,256]{2,1,0:T(8,128)S(1)} fusion(f32[2,4160,256]{2,1,0:T(8,128)} %all-gather.5.cloned.1.call-done, f32[520,4160]{1,0:T(8,128)} %concatenate.62), kind=kOutput, calls=%fused_computation.88 | convolution fusion | flops 6645350400 | bytes 18237440 | tf_op jit(solution)/shard_map/ik,rkj->rij/dot_general | solution.py:125
  233.5 4.9 %collective-permute-start.6 = (f32[2,520,2]{1,2,0:T(2,128)S(1)}, f32[2,520,2]{1,2,0:T(2,128)S(1)}, u32[]{:S(2)}, u32[]{:S(2)}) collective-permute-start(f32[2,520,2]{1,2,0:T(2,128)S(1)} %copy.10), channel_id=1, source_target_pairs={{0,1},{1,2},{2,3},{3,4},{4,5},{5,6},{6,7},{7,8},{8,9},{9,10},{10,1... | collective-permute-start | bytes 24968 | tf_op jit(solution)/shard_map/ppermute | solution.py:19
  238.7 2.1 collective-permute-start.7
  241.4 3.1 %collective-permute-done.7 = f32[2,520,2]{1,2,0:T(2,128)S(1)} collective-permute-done((f32[2,520,2]{1,2,0:T(2,128)S(1)}, f32[2,520,2]{1,2,0:T(2,128)S(1)}, u32[]{:S(2)}, u32[]{:S(2)}) %collective-permute-start.7) | collective-permute-done | bytes 8352 | tf_op jit(solution)/shard_map/ppermute | solution.py:21
  246.0 2.5 reduce-precision_convert_fusion.3
  248.9 4.0 %multiply_add_fusion = f32[2,1024,512]{2,1,0:T(8,128)} fusion(f32[2,1024,512]{2,1,0:T(8,128)S(1)} %copy-done.1, f32[1024,512]{1,0:T(8,128)S(1)} %copy-done.7, bf16[2,1024,260]{1,2,0:T(8,128)(2,1)S(1)} %get-tuple-element.29, bf16[2,1024,260]{1,2,0:T(8,128)(2,1)S(1)} %get-tuple-element.30, bf16[2,1024,260]{1,2,0:T(8,128)(2,1)S(1)} %get-tuple-element.28, ...), kind=kOutput, calls=%fused_computation.20 | convolution fusion | flops 1649856512 | bytes 13946880 | tf_op jit(solution)/shard_map/rpj,jq->rpq/dot_general | solution.py:72
  (53 shorter events, 12.8 us)
Async XLA Ops:
  6.5 73.2 %all-gather.3.cloned.1.call-start = ((), (), s32[]{:S(2)}) async-start(), calls=%async_computation | async-start | bytes 9584640 | tf_op jit(solution)/shard_map/all_gather | solution.py:121
  8.8 10.8 %collective-permute-start = (f32[2,1024,4]{1,2,0:T(4,128)S(1)}, f32[2,1024,4]{1,2,0:T(4,128)S(1)}, u32[]{:S(2)}, u32[]{:S(2)}) collective-permute-start(f32[2,1024,4]{1,2,0:T(4,128)S(1)} %copy.16), channel_id=1, source_target_pairs={{0,1},{1,2},{2,3},{3,4},{4,5},{5,6},{6,7},{7,8},{8,9},{9,10},{10,1... | collective-permute-start | bytes 98312 | tf_op jit(solution)/shard_map/ppermute | solution.py:33
  12.7 7.4 %collective-permute-start.1 = (f32[2,1024,4]{1,2,0:T(4,128)S(1)}, f32[2,1024,4]{1,2,0:T(4,128)S(1)}, u32[]{:S(2)}, u32[]{:S(2)}) collective-permute-start(f32[2,1024,4]{1,2,0:T(4,128)S(1)} %copy.17), channel_id=1, source_target_pairs={{1,0},{2,1},{3,2},{4,3},{5,4},{6,5},{7,6},{8,7},{9,8},{10,9},{11,1... | collective-permute-start | bytes 98312 | tf_op jit(solution)/shard_map/ppermute | solution.py:34
  25.7 195.2 %all-gather.5.cloned.1.call-start = ((), (), s32[]{:S(2)}) async-start(), calls=%async_computation.1 | async-start | bytes 9584640 | tf_op jit(solution)/shard_map/all_gather | solution.py:128
  28.4 0.8 copy-start.2
  28.4 1.0 copy-start.4
  29.3 46.5 %collective-permute-start.2 = (f32[256,2048]{1,0:T(8,128)S(1)}, f32[256,2048]{1,0:T(8,128)}, u32[]{:S(2)}, u32[]{:S(2)}) collective-permute-start(f32[256,2048]{1,0:T(8,128)S(1)} %fusion.65), channel_id=1, source_target_pairs={{0,2},{2,0},{1,3},{3,1},{4,6},{6,4},{5,7},{7,5},{8,10},{10,8},{9,1... | collective-permute-start | bytes 6291464 | tf_op jit(solution)/shard_map/ppermute | solution.py:106
  79.8 7.4 %copy-start = (f32[2,520,2048]{2,1,0:T(8,128)S(1)}, f32[2,520,2048]{2,1,0:T(8,128)}, u32[]{:S(2)}) copy-start(f32[2,520,2048]{2,1,0:T(8,128)} %all-gather.3.cloned.1.call-done) | copy-start | bytes 25559044
  79.8 7.4 %copy-start.3 = (f32[256,512]{1,0:T(8,128)S(1)}, f32[256,512]{1,0:T(8,128)}, u32[]{:S(2)}) copy-start(f32[256,512]{1,0:T(8,128)} %copy-done.2) | copy-start | bytes 1572868
  79.8 7.4 %copy-start.5 = (f32[256,512]{1,0:T(8,128)S(1)}, f32[256,512]{1,0:T(8,128)}, u32[]{:S(2)}) copy-start(f32[256,512]{1,0:T(8,128)} %copy-done.4) | copy-start | bytes 1572868
  86.7 25.1 %collective-permute-start.3 = (f32[2,520,256]{2,1,0:T(8,128)S(1)}, f32[2,520,256]{2,1,0:T(8,128)S(1)}, u32[]{:S(2)}, u32[]{:S(2)}) collective-permute-start(f32[2,520,256]{2,1,0:T(8,128)S(1)} %fusion.49), channel_id=1, source_target_pairs={{0,2},{2,0},{1,3},{3,1},{4,6},{6,4},{5,7},{7,5},{8,10},{10,8},{9,1... | collective-permute-start | bytes 3194888 | tf_op jit(solution)/shard_map/ppermute | solution.py:124
  114.0 6.8 %collective-permute-start.4 = (f32[2,4096]{1,0:T(2,128)S(1)}, f32[2,4096]{1,0:T(2,128)S(1)}, u32[]{:S(2)}, u32[]{:S(2)}) collective-permute-start(f32[2,4096]{1,0:T(2,128)S(1)} %get-tuple-element.13), channel_id=1, source_target_pairs={{0,16},{16,32},{32,48},{48,64},{64,80},{80,96},{96,112},{1,17},{17... | collective-permute-start | bytes 98312 | tf_op jit(solution)/shard_map/ppermute | solution.py:19
  117.2 4.7 %collective-permute-start.5 = (f32[2,4096]{1,0:T(2,128)S(1)}, f32[2,4096]{1,0:T(2,128)S(1)}, u32[]{:S(2)}, u32[]{:S(2)}) collective-permute-start(f32[2,4096]{1,0:T(2,128)S(1)} %get-tuple-element.14), channel_id=1, source_target_pairs={{16,0},{32,16},{48,32},{64,48},{80,64},{96,80},{112,96},{17,1},{33... | collective-permute-start | bytes 98312 | tf_op jit(solution)/shard_map/ppermute | solution.py:21
  233.5 7.7 %collective-permute-start.6 = (f32[2,520,2]{1,2,0:T(2,128)S(1)}, f32[2,520,2]{1,2,0:T(2,128)S(1)}, u32[]{:S(2)}, u32[]{:S(2)}) collective-permute-start(f32[2,520,2]{1,2,0:T(2,128)S(1)} %copy.10), channel_id=1, source_target_pairs={{0,1},{1,2},{2,3},{3,4},{4,5},{5,6},{6,7},{7,8},{8,9},{9,10},{10,1... | collective-permute-start | bytes 24968 | tf_op jit(solution)/shard_map/ppermute | solution.py:19
  238.7 5.9 %collective-permute-start.7 = (f32[2,520,2]{1,2,0:T(2,128)S(1)}, f32[2,520,2]{1,2,0:T(2,128)S(1)}, u32[]{:S(2)}, u32[]{:S(2)}) collective-permute-start(f32[2,520,2]{1,2,0:T(2,128)S(1)} %copy.11), channel_id=1, source_target_pairs={{1,0},{2,1},{3,2},{4,3},{5,4},{6,5},{7,6},{8,7},{9,8},{10,9},{11,1... | collective-permute-start | bytes 24968 | tf_op jit(solution)/shard_map/ppermute | solution.py:21
  244.8 1.2 copy-start.6
  246.0 2.5 copy-start.1
  246.0 2.9 %copy-start.7 = (f32[1024,512]{1,0:T(8,128)S(1)}, f32[1024,512]{1,0:T(8,128)}, u32[]{:S(2)}) copy-start(f32[1024,512]{1,0:T(8,128)} %param.5) | copy-start | bytes 6291460
Sparse Core Ops, SparseCore 0:
  25.8 53.9 all-gather.2
  113.1 107.7 all-gather.4
where the time goes:
time: 260 us
  waiting for transfers between devices  149 us (57%)
  matrix products  35.2 us (14%)
  local copies, waits for them, and re-layouts  23.9 us (9%)
  other arithmetic  20.5 us (8%)
  starting transfers between devices  17.9 us (7%)
  between operations  13.7 us (5%)
    all_gather x1, waiting for transfers between devices, body(): lax.all_gather(mixed, ('z', 'yh'), axis=1, tiled=True)  73.1 us
    ppermute x1, waiting for transfers between devices, body(): partner_cols = lax.ppermute(far_cols, 'yl', swap)  46.2 us
    ppermute x1, waiting for transfers between devices, body(): mixed = near + lax.ppermute(for_partner, 'yl', swap)  21.1 us
    dot_general x1, matrix products, body(): jnp.einsum('ik,rkj->rij', row_big, lax.all_gather(mixed, ('z', 'yh'), axi...  12.2 us
    concatenate x1, local copies, waits for them, and re-layouts, row_windows(): jnp.concatenate([padded[:, block * w:block * w + width] for w in order],...  11.6 us
    concatenate x1, other arithmetic, with_halo(): jnp.concatenate([lax.ppermute(tail, axis, [(i, (i + 1) % count) for i in...  10.9 us
    ppermute x2, starting transfers between devices, with_halo(): lax.ppermute(tail, axis, [(i, (i + 1) % count) for i in range(ends)])  8.12 us
    dot_general x4, matrix products, exact_dot(): jnp.einsum(eq, parts, jnp.concatenate([table] * 3, axis=0), preferred_ele...  7.22 us
  transfers between devices with their start and end apart: 10, of which 6 were waited for; matrix products, arithmetic and copies ran while one was open for 16% of the time, Pallas kernels for 0%

commit v1 on v0

--- a/solution.py
+++ b/solution.py
@@ -125,7 +125,10 @@
     product = jnp.einsum(
         "ik,rkj->rij",
         row_big,
-        lax.all_gather(mixed, ("z", "yh"), axis=1, tiled=True),
+        jnp.concatenate(
+            lax.all_to_all(jnp.stack([mixed] * lax.axis_size(("z", "yh"))), ("z", "yh"), 0, 0),
+            axis=1,
+        ),
         precision=highest,
     )
     coarse_ext = with_halo(product, ((cols_axis, 2),), 2)

time: 260 us -> 283 us (1.088)
  waiting for transfers between devices: 149 us -> 160 us
  local copies, waits for them, and re-layouts: 23.9 us -> 33.9 us
  starting transfers between devices: 17.9 us -> 23.8 us
  matrix products: 35.2 us -> 30.6 us
    all_gather x1 -> x0, waiting for transfers between devices: 73.1 us -> none  [body(): lax.all_gather(mixed, ('z', 'yh'), axis=1, tiled=True)]
    ppermute x2, waiting for transfers between devices: 0.01 us -> 60.3 us  [with_halo(): lax.ppermute(tail, axis, [(i, (i + 1) % count) for i in range(ends)])]
    ppermute x2, waiting for transfers between devices: 4.19 us -> 28.2 us  [with_halo(): lax.ppermute(head, axis, [((i + 1) % count, i) for i in range(ends)])]
    all_to_all x0 -> x1, starting transfers between devices: none -> 5.7 us  [body(): lax.all_to_all(jnp.stack([mixed] * lax.axis_size(('z', 'yh'))), ('z', 'yh...]
    dot_general x1, matrix products: 12.2 us -> 7.59 us  [body(): jnp.einsum('ik,rkj->rij', row_big, jnp.concatenate(lax.all_to_all(jnp.sta...]
    reshape x0 -> x1, local copies, waits for them, and re-layouts: none -> 4.34 us  [body(): jnp.concatenate(lax.all_to_all(jnp.stack([mixed] * lax.axis_size(('z', 'y...]
    another operation x0 -> x1, local copies, waits for them, and re-layouts: none -> 4.18 us  [body(): jnp.stack([mixed] * lax.axis_size(('z', 'yh')))]
  transfers between devices with their start and end apart: 10 -> 10, of which waited for: 6 -> 6; matrix products, arithmetic and copies ran while one was open for 16% -> 15% of each run, Pallas kernels for 0% -> 0%
where the time goes in v1:
time: 283 us; the launch traced here: 281 us
  waiting for transfers between devices  160 us (57%)
  local copies, waits for them, and re-layouts  33.9 us (12%)
  matrix products  30.6 us (11%)
  starting transfers between devices  23.8 us (8%)
  other arithmetic  19.4 us (7%)
  between operations  13.7 us (5%)
    ppermute x2, waiting for transfers between devices, with_halo(): lax.ppermute(tail, axis, [(i, (i + 1) % count) for i in range(ends)])  60.3 us
    ppermute x1, waiting for transfers between devices, body(): partner_cols = lax.ppermute(far_cols, 'yl', swap)  46.2 us
    ppermute x2, waiting for transfers between devices, with_halo(): lax.ppermute(head, axis, [((i + 1) % count, i) for i in range(ends)])  28.2 us
    ppermute x1, waiting for transfers between devices, body(): mixed = near + lax.ppermute(for_partner, 'yl', swap)  21.1 us
    concatenate x1, local copies, waits for them, and re-layouts, row_windows(): jnp.concatenate([padded[:, block * w:block * w + width] for w in order],...  11.6 us
    concatenate x1, other arithmetic, with_halo(): jnp.concatenate([lax.ppermute(tail, axis, [(i, (i + 1) % count) for i in...  10.7 us
    ppermute x2, starting transfers between devices, with_halo(): lax.ppermute(tail, axis, [(i, (i + 1) % count) for i in range(ends)])  8.59 us
    dot_general x1, matrix products, body(): jnp.einsum('ik,rkj->rij', row_big, jnp.concatenate(lax.all_to_all(jnp.sta...  7.59 us
  transfers between devices with their start and end apart: 10, of which 6 were waited for; matrix products, arithmetic and copies ran while one was open for 15% of the time, Pallas kernels for 0%

profile of v1, /device:TPU:9, one launch (start us, length us, event | category | flops | bytes accessed | tf_op | source)
XLA Modules:
  0.0 281.2 jit_solution(1481416574945295032)
XLA Ops:
  8.8 3.6 %collective-permute-start = (f32[2,1024,4]{1,2,0:T(4,128)S(1)}, f32[2,1024,4]{1,2,0:T(4,128)S(1)}, u32[]{:S(2)}, u32[]{:S(2)}) collective-permute-start(f32[2,1024,4]{1,2,0:T(4,128)S(1)} %copy.17), channel_id=1, source_target_pairs={{0,1},{1,2},{2,3},{3,4},{4,5},{5,6},{6,7},{7,8},{8,9},{9,10},{10,1... | collective-permute-start | bytes 98312 | tf_op jit(solution)/shard_map/ppermute | solution.py:33
  14.6 3.2 %reduce-precision_convert_fusion.1 = (bf16[2,1024,512]{2,1,0:T(8,128)(2,1)S(1)}, bf16[2,1024,512]{2,1,0:T(8,128)(2,1)S(1)}, bf16[2,1024,512]{2,1,0:T(8,128)(2,1)S(1)}) fusion(f32[2,1024,512]{2,1,0:T(8,128)} %param.4), kind=kLoop, calls=%fused_computation.18 | loop fusion | flops 7340032 | bytes 10485760 | tf_op jit(solution)/shard_map/convert_element_type | solution.py:64
  22.9 2.8 fusion.59
  25.7 2.6 fusion.116
  29.7 46.2 %collective-permute-done.2 = f32[256,2048]{1,0:T(8,128)} collective-permute-done((f32[256,2048]{1,0:T(8,128)S(1)}, f32[256,2048]{1,0:T(8,128)}, u32[]{:S(2)}, u32[]{:S(2)}) %collective-permute-start.2) | collective-permute-done | bytes 2097184 | tf_op jit(solution)/shard_map/ppermute | solution.py:106
  75.8 4.0 %all-gather.2.cloned.1.call-done = f32[2,520,2048]{2,1,0:T(8,128)} async-done(((f32[2,520,256]{2,1,0:T(8,128)}), f32[2,520,2048]{2,1,0:T(8,128)}) %all-gather.2.cloned.1.call-update) | async-done | bytes 8519696 | tf_op jit(solution)/shard_map/all_gather | solution.py:121
  79.8 6.9 %fusion.49 = f32[2,520,256]{2,1,0:T(8,128)S(1)} fusion(f32[2,520,2048]{2,1,0:T(8,128)} %all-gather.2.cloned.1.call-done, f32[256,2048]{1,0:T(8,128)} %collective-permute-done.2), kind=kOutput, calls=%fused_computation.79 | convolution fusion | flops 3271557120 | bytes 11681792 | tf_op jit(solution)/shard_map/rik,jk->rij/dot_general | solution.py:123
  87.2 3.5 %fusion.51 = f32[2,520,256]{2,1,0:T(8,128)S(1)} fusion(f32[2,520,2048]{2,1,0:T(8,128)S(1)} %copy-done.1, f32[256,512]{1,0:T(8,128)S(1)} %copy-done.4, f32[256,512]{1,0:T(8,128)S(1)} %copy-done.6, f32[256,512]{1,0:T(8,128)S(1)} %get-tuple-element.16, f32[256,512]{1,0:T(8,128)S(1)} %get-tuple-element.17, f32[256,512]{1,0:T(8,128)S(1)} %get-tuple-element.18, ...), kind=kOutput, calls=%fused_computation.81 | convolution fusion | flops 3275227136 | bytes 13778945 | tf_op jit(solution)/shard_map/rik,jk->rij/dot_general | solution.py:122
  90.7 21.1 %collective-permute-done.3 = f32[2,520,256]{2,1,0:T(8,128)S(1)} collective-permute-done((f32[2,520,256]{2,1,0:T(8,128)S(1)}, f32[2,520,256]{2,1,0:T(8,128)S(1)}, u32[]{:S(2)}, u32[]{:S(2)}) %collective-permute-start.3) | collective-permute-done | bytes 1064992 | tf_op jit(solution)/shard_map/ppermute | solution.py:124
  112.0 4.2 %stack.2 = f32[8,2,520,256]{3,2,1,0:T(8,128)} broadcast(f32[2,520,256]{2,1,0:T(8,128)S(1)} %add.216), dimensions={1,2,3} | broadcast | bytes 9584640 | tf_op jit(solution)/shard_map/stack | solution.py:129
  116.2 5.7 %all-to-all-start = ((f32[8,2,520,256]{3,2,1,0:T(8,128)}), f32[8,2,520,256]{3,2,1,0:T(8,128)}, u32[]{:S(2)}, u32[]{:S(2)}) async-start(f32[8,2,520,256]{3,2,1,0:T(8,128)} %stack.2), calls=%async_computation | async-start | bytes 17039360 | tf_op jit(solution)/shard_map/all_to_all | solution.py:129
  122.8 3.4 %collective-permute-start.4 = (f32[2,4096]{1,0:T(2,128)S(1)}, f32[2,4096]{1,0:T(2,128)S(1)}, u32[]{:S(2)}, u32[]{:S(2)}) collective-permute-start(f32[2,4096]{1,0:T(2,128)S(1)} %get-tuple-element.13), channel_id=1, source_target_pairs={{0,16},{16,32},{32,48},{48,64},{64,80},{80,96},{96,112},{1,17},{17... | collective-permute-start | bytes 98312 | tf_op jit(solution)/shard_map/ppermute | solution.py:19
  127.5 2.3 fusion.43
  129.8 60.3 %collective-permute-done.4 = f32[2,4096]{1,0:T(2,128)S(1)} collective-permute-done((f32[2,4096]{1,0:T(2,128)S(1)}, f32[2,4096]{1,0:T(2,128)S(1)}, u32[]{:S(2)}, u32[]{:S(2)}) %collective-permute-start.4) | collective-permute-done | bytes 32800 | tf_op jit(solution)/shard_map/ppermute | solution.py:19
  190.1 24.8 %collective-permute-done.5 = f32[2,4096]{1,0:T(2,128)S(1)} collective-permute-done((f32[2,4096]{1,0:T(2,128)S(1)}, f32[2,4096]{1,0:T(2,128)S(1)}, u32[]{:S(2)}, u32[]{:S(2)}) %collective-permute-start.5) | collective-permute-done | bytes 32800 | tf_op jit(solution)/shard_map/ppermute | solution.py:21
  215.0 10.7 %select_maximum_fusion = f32[520,4104]{1,0:T(8,128)S(1)} fusion(f32[2,4096]{1,0:T(2,128)S(1)} %collective-permute-done.5, f32[512,4096]{1,0:T(8,128)} %param.6, f32[2,4096]{1,0:T(2,128)S(1)} %collective-permute-done.4), kind=kLoop, calls=%fused_computation.2 | loop fusion | flops 27743040 | bytes 16990464 | tf_op jit(solution)/shard_map/concatenate | solution.py:17
  225.7 3.3 %fusion.114 = (f32[520,520]{1,0:T(8,128)S(1)}, f32[520,520]{1,0:T(8,128)S(1)}, f32[520,520]{1,0:T(8,128)}, f32[520,520]{1,0:T(8,128)}, f32[520,520]{1,0:T(8,128)...) fusion(f32[520,4104]{1,0:T(8,128)S(1)} %select_maximum_fusion), kind=kLoop, calls=%fused_computation.159 | loop fusion | bytes 17305600 | tf_op jit(solution)/shard_map/slice | solution.py:83
  229.1 11.6 %concatenate.62 = f32[520,4160]{1,0:T(8,128)} concatenate(f32[520,520]{1,0:T(8,128)} %get-tuple-element.12, f32[520,520]{1,0:T(8,128)} %get-tuple-element.11, f32[520,520]{1,0:T(8,128)} %get-tuple-element.10, f32[520,520]{1,0:T(8,128)} %get-tuple-element.9, f32[520,520]{1,0:T(8,128)} %get-tuple-element.8, f32[520,520]{1,0:T(8,128)} %get-tuple-element.7, ...), dimensions={1} | concatenate | bytes 17305600 | tf_op jit(solution)/shard_map/concatenate | solution.py:83
  240.7 4.3 %copy.10 = f32[2,8,520,256]{3,2,1,0:T(8,128)S(1)} copy(f32[2,8,520,256]{3,2,0,1:T(8,128)} %bitcast.7) | data formatting | bytes 17039360 | tf_op jit(solution)/shard_map/reshape | solution.py:128
  246.6 7.6 %fusion.62 = f32[2,520,256]{2,1,0:T(8,128)S(1)} fusion(f32[2,4160,256]{2,1,0:T(8,128)S(1)} %bitcast.51, f32[520,4160]{1,0:T(8,128)S(1)} %copy-done), kind=kOutput, calls=%fused_computation.88 | convolution fusion | flops 6645350400 | bytes 18237440 | tf_op jit(solution)/shard_map/ik,rkj->rij/dot_general | solution.py:125
  254.6 5.2 %collective-permute-start.6 = (f32[2,520,2]{1,2,0:T(2,128)S(1)}, f32[2,520,2]{1,2,0:T(2,128)S(1)}, u32[]{:S(2)}, u32[]{:S(2)}) collective-permute-start(f32[2,520,2]{1,2,0:T(2,128)S(1)} %copy.11), channel_id=1, source_target_pairs={{0,1},{1,2},{2,3},{3,4},{4,5},{5,6},{6,7},{7,8},{8,9},{9,10},{10,1... | collective-permute-start | bytes 24968 | tf_op jit(solution)/shard_map/ppermute | solution.py:19
  262.7 3.3 %collective-permute-done.7 = f32[2,520,2]{1,2,0:T(2,128)S(1)} collective-permute-done((f32[2,520,2]{1,2,0:T(2,128)S(1)}, f32[2,520,2]{1,2,0:T(2,128)S(1)}, u32[]{:S(2)}, u32[]{:S(2)}) %collective-permute-start.7) | collective-permute-done | bytes 8352 | tf_op jit(solution)/shard_map/ppermute | solution.py:21
  267.5 2.5 reduce-precision_convert_fusion.3
  270.3 4.0 %multiply_add_fusion = f32[2,1024,512]{2,1,0:T(8,128)} fusion(f32[2,1024,512]{2,1,0:T(8,128)S(1)} %copy-done.2, f32[1024,512]{1,0:T(8,128)S(1)} %copy-done.8, bf16[2,1024,260]{1,2,0:T(8,128)(2,1)S(1)} %get-tuple-element.29, bf16[2,1024,260]{1,2,0:T(8,128)(2,1)S(1)} %get-tuple-element.30, bf16[2,1024,260]{1,2,0:T(8,128)(2,1)S(1)} %get-tuple-element.28, ...), kind=kOutput, calls=%fused_computation.20 | convolution fusion | flops 1649856512 | bytes 13946880 | tf_op jit(solution)/shard_map/rpj,jq->rpq/dot_general | solution.py:72
  (56 shorter events, 20.3 us)
Async XLA Ops:
  6.5 73.2 %all-gather.2.cloned.1.call-start = ((), (), s32[]{:S(2)}) async-start(), calls=%async_computation.1 | async-start | bytes 9584640 | tf_op jit(solution)/shard_map/all_gather | solution.py:121
  8.8 10.8 %collective-permute-start = (f32[2,1024,4]{1,2,0:T(4,128)S(1)}, f32[2,1024,4]{1,2,0:T(4,128)S(1)}, u32[]{:S(2)}, u32[]{:S(2)}) collective-permute-start(f32[2,1024,4]{1,2,0:T(4,128)S(1)} %copy.17), channel_id=1, source_target_pairs={{0,1},{1,2},{2,3},{3,4},{4,5},{5,6},{6,7},{7,8},{8,9},{9,10},{10,1... | collective-permute-start | bytes 98312 | tf_op jit(solution)/shard_map/ppermute | solution.py:33
  12.7 7.4 %collective-permute-start.1 = (f32[2,1024,4]{1,2,0:T(4,128)S(1)}, f32[2,1024,4]{1,2,0:T(4,128)S(1)}, u32[]{:S(2)}, u32[]{:S(2)}) collective-permute-start(f32[2,1024,4]{1,2,0:T(4,128)S(1)} %copy.18), channel_id=1, source_target_pairs={{1,0},{2,1},{3,2},{4,3},{5,4},{6,5},{7,6},{8,7},{9,8},{10,9},{11,1... | collective-permute-start | bytes 98312 | tf_op jit(solution)/shard_map/ppermute | solution.py:34
  28.3 0.8 copy-start.3
  28.3 1.0 copy-start.5
  29.3 46.5 %collective-permute-start.2 = (f32[256,2048]{1,0:T(8,128)S(1)}, f32[256,2048]{1,0:T(8,128)}, u32[]{:S(2)}, u32[]{:S(2)}) collective-permute-start(f32[256,2048]{1,0:T(8,128)S(1)} %fusion.65), channel_id=1, source_target_pairs={{0,2},{2,0},{1,3},{3,1},{4,6},{6,4},{5,7},{7,5},{8,10},{10,8},{9,1... | collective-permute-start | bytes 6291464 | tf_op jit(solution)/shard_map/ppermute | solution.py:106
  79.8 7.4 %copy-start.1 = (f32[2,520,2048]{2,1,0:T(8,128)S(1)}, f32[2,520,2048]{2,1,0:T(8,128)}, u32[]{:S(2)}) copy-start(f32[2,520,2048]{2,1,0:T(8,128)} %all-gather.2.cloned.1.call-done) | copy-start | bytes 25559044
  79.8 7.4 %copy-start.4 = (f32[256,512]{1,0:T(8,128)S(1)}, f32[256,512]{1,0:T(8,128)}, u32[]{:S(2)}) copy-start(f32[256,512]{1,0:T(8,128)} %copy-done.3) | copy-start | bytes 1572868
  79.8 7.4 %copy-start.6 = (f32[256,512]{1,0:T(8,128)S(1)}, f32[256,512]{1,0:T(8,128)}, u32[]{:S(2)}) copy-start(f32[256,512]{1,0:T(8,128)} %copy-done.5) | copy-start | bytes 1572868
  86.7 25.1 %collective-permute-start.3 = (f32[2,520,256]{2,1,0:T(8,128)S(1)}, f32[2,520,256]{2,1,0:T(8,128)S(1)}, u32[]{:S(2)}, u32[]{:S(2)}) collective-permute-start(f32[2,520,256]{2,1,0:T(8,128)S(1)} %fusion.49), channel_id=1, source_target_pairs={{0,2},{2,0},{1,3},{3,1},{4,6},{6,4},{5,7},{7,5},{8,10},{10,8},{9,1... | collective-permute-start | bytes 3194888 | tf_op jit(solution)/shard_map/ppermute | solution.py:124
  116.2 124.5 %all-to-all-start = ((f32[8,2,520,256]{3,2,1,0:T(8,128)}), f32[8,2,520,256]{3,2,1,0:T(8,128)}, u32[]{:S(2)}, u32[]{:S(2)}) async-start(f32[8,2,520,256]{3,2,1,0:T(8,128)} %stack.2), calls=%async_computation | async-start | bytes 17039360 | tf_op jit(solution)/shard_map/all_to_all | solution.py:129
  122.8 67.3 %collective-permute-start.4 = (f32[2,4096]{1,0:T(2,128)S(1)}, f32[2,4096]{1,0:T(2,128)S(1)}, u32[]{:S(2)}, u32[]{:S(2)}) collective-permute-start(f32[2,4096]{1,0:T(2,128)S(1)} %get-tuple-element.13), channel_id=1, source_target_pairs={{0,16},{16,32},{32,48},{48,64},{64,80},{80,96},{96,112},{1,17},{17... | collective-permute-start | bytes 98312 | tf_op jit(solution)/shard_map/ppermute | solution.py:19
  126.2 88.8 %collective-permute-start.5 = (f32[2,4096]{1,0:T(2,128)S(1)}, f32[2,4096]{1,0:T(2,128)S(1)}, u32[]{:S(2)}, u32[]{:S(2)}) collective-permute-start(f32[2,4096]{1,0:T(2,128)S(1)} %get-tuple-element.14), channel_id=1, source_target_pairs={{16,0},{32,16},{48,32},{64,48},{80,64},{96,80},{112,96},{17,1},{33... | collective-permute-start | bytes 98312 | tf_op jit(solution)/shard_map/ppermute | solution.py:21
  240.7 5.9 %copy-start = (f32[520,4160]{1,0:T(8,128)S(1)}, f32[520,4160]{1,0:T(8,128)}, u32[]{:S(2)}) copy-start(f32[520,4160]{1,0:T(8,128)} %concatenate.62) | copy-start | bytes 25958404
  254.6 7.8 %collective-permute-start.6 = (f32[2,520,2]{1,2,0:T(2,128)S(1)}, f32[2,520,2]{1,2,0:T(2,128)S(1)}, u32[]{:S(2)}, u32[]{:S(2)}) collective-permute-start(f32[2,520,2]{1,2,0:T(2,128)S(1)} %copy.11), channel_id=1, source_target_pairs={{0,1},{1,2},{2,3},{3,4},{4,5},{5,6},{6,7},{7,8},{8,9},{9,10},{10,1... | collective-permute-start | bytes 24968 | tf_op jit(solution)/shard_map/ppermute | solution.py:19
  260.1 5.9 %collective-permute-start.7 = (f32[2,520,2]{1,2,0:T(2,128)S(1)}, f32[2,520,2]{1,2,0:T(2,128)S(1)}, u32[]{:S(2)}, u32[]{:S(2)}) collective-permute-start(f32[2,520,2]{1,2,0:T(2,128)S(1)} %copy.12), channel_id=1, source_target_pairs={{1,0},{2,1},{3,2},{4,3},{5,4},{6,5},{7,6},{8,7},{9,8},{10,9},{11,1... | collective-permute-start | bytes 24968 | tf_op jit(solution)/shard_map/ppermute | solution.py:21
  266.2 1.2 copy-start.7
  267.5 2.5 copy-start.2
  267.5 2.9 %copy-start.8 = (f32[1024,512]{1,0:T(8,128)S(1)}, f32[1024,512]{1,0:T(8,128)}, u32[]{:S(2)}) copy-start(f32[1024,512]{1,0:T(8,128)} %param.5) | copy-start | bytes 6291460
Sparse Core Ops, SparseCore 0:
  25.8 53.9 all-gather.1
